TPU v7x, 128 devices: a whole 4x4x4 slice. The times are simulated.
128 devices in a mesh: req: 16 (over z, x), exp: 8 (over y, core).
Axes of the slice: x: 4, y: 4, z: 4, core: 2. Of those that a mesh axis runs over, the one named last changes fastest.
Arguments:
- tokens: bfloat16 [12288, 2880], P(('req', 'exp')), may hold values from -6 to 6
- attn_gain: float32 [2880], replicated, may hold values from 0.5 to 8
- w_query: bfloat16 [2880, 4096], P(None, 'exp'), may hold values from -0.109375 to 0.109375
- key_weight: bfloat16 [2880, 512], P(None, 'exp'), may hold values from -0.109375 to 0.109375
- value_weight: bfloat16 [2880, 512], P(None, 'exp'), may hold values from -0.109375 to 0.109375
- sinks: float32 [64], P('exp'), may hold values from -1 to 3
- w_out: bfloat16 [4096, 2880], P('exp'), may hold values from -0.09375 to 0.09375
- ffn_gain: float32 [2880], replicated, may hold values from 0.25 to 1.75
- router: bfloat16 [2880, 32], replicated, may hold values from -0.109375 to 0.109375
- routes: int32 [12288, 4], P(('req', 'exp')), may hold values from 0 to 31, all different within a row; in each aligned block of 96 rows (0 to 95, 96 to 191, ...) at most 14 rows name the same one
- lengths: int32 [16, 6], P('req'), may hold values from 1 to 384, 768 in all within a row
- expert_gate: bfloat16 [128, 2880, 720], P(('req', 'exp')), may hold values from -0.109375 to 0.109375
- expert_up: bfloat16 [128, 2880, 720], P(('req', 'exp')), may hold values from -0.109375 to 0.109375
- expert_down: bfloat16 [128, 720, 2880], P(('req', 'exp')), may hold values from -0.109375 to 0.109375
Outputs:
- layer_out: bfloat16 [12288, 2880], P(('req', 'exp'))
Inputs may be any that keep to these rules, and one draw needn't show every extreme that they name: `routes`: in the rows of one device no expert is named by more than 14 rows, a bound that some block reaches; a row names 4 different experts.
All inputs are finite; a program needn't handle non-finite values.
Results may differ from a plain program's by a relative error of at most 0.02.
The roundings to bfloat16 on the way count: a program that leaves them out, or rounds other values in their place, can miss the bound.
Values may be sent and summed in bfloat16 or wider, within the bound.
No kernel may reach another device: no remote copies, remote signals or barrier semaphores. Data moves between devices by JAX's collectives and lax.ppermute only.
A program may use at most 192 MiB of HBM per device.

v0:
```python
import jax
import jax.numpy as jnp
from jax import lax
from jax.sharding import PartitionSpec as P

QUERY_HEADS = 64
KEY_VALUE_HEADS = 8
HEAD_DIM = 64
EXPERTS = 32
TOPK = 4
CAP = 14


def rms_norm(value_rows, gain):
    mean_sq = jnp.mean(value_rows * value_rows, axis=-1, keepdims=True)
    return value_rows * lax.rsqrt(mean_sq + 1e-05) * gain


def rotate(value_rows, offset):
    half = value_rows.shape[-1] // 2
    freqs = jnp.exp(
        -(2.0 * jnp.arange(half, dtype=jnp.float32) / value_rows.shape[-1])
        * jnp.log(jnp.float32(150000.0))
    )
    angle = offset.astype(jnp.float32)[:, None] * freqs[None, :]
    cosine = jnp.cos(angle)[:, None, :]
    sine = jnp.sin(angle)[:, None, :]
    first = value_rows[..., :half]
    second = value_rows[..., half:]
    return jnp.concatenate(
        [first * cosine - second * sine, second * cosine + first * sine], axis=-1
    )


def per_device(
    tokens,
    attn_gain,
    w_query,
    key_weight,
    value_weight,
    sinks,
    w_out,
    ffn_gain,
    router,
    routes,
    lengths,
    expert_gate,
    expert_up,
    expert_down,
):
    tok_rows = tokens.shape[0]
    model_width = tokens.shape[1]
    local_heads = w_query.shape[1] // HEAD_DIM
    local_kv = key_weight.shape[1] // HEAD_DIM
    head_group = QUERY_HEADS // KEY_VALUE_HEADS
    normed_input = rms_norm(tokens.astype(jnp.float32), attn_gain).astype(jnp.bfloat16)
    by_chip = lax.all_gather(normed_input, "y", axis=0, tiled=False)
    piece = lax.all_gather(by_chip, "c", axis=1, tiled=True).reshape(-1, model_width)
    projected = jnp.concatenate(
        [
            jnp.dot(piece, w_query, preferred_element_type=jnp.float32),
            jnp.dot(piece, key_weight, preferred_element_type=jnp.float32),
            jnp.dot(piece, value_weight, preferred_element_type=jnp.float32),
        ],
        axis=1,
    )
    item_count = projected.shape[0]
    lens = lengths[0]
    ends = jnp.cumsum(lens)
    starts = ends - lens
    position = jnp.arange(item_count, dtype=jnp.int32)
    member = ((position[:, None] >= starts[None, :]) & (position[:, None] < ends[None, :])).astype(
        jnp.int32
    )
    segment = jnp.sum(member * jnp.arange(lens.shape[0], dtype=jnp.int32)[None, :], axis=1)
    offset = position - jnp.sum(member * starts[None, :], axis=1)
    q_width = local_heads * HEAD_DIM
    kv_width = local_kv * HEAD_DIM
    query_rows = rotate(
        projected[:, :q_width].reshape(item_count, local_heads, HEAD_DIM), offset
    ).astype(jnp.bfloat16)
    key_rows = rotate(
        projected[:, q_width : q_width + kv_width].reshape(item_count, local_kv, HEAD_DIM), offset
    ).astype(jnp.bfloat16)
    value_rows = (
        projected[:, q_width + kv_width :]
        .reshape(item_count, local_kv, HEAD_DIM)
        .astype(jnp.bfloat16)
    )
    grouped_heads = query_rows.reshape(item_count, local_kv, head_group, HEAD_DIM)
    scores = jnp.einsum(
        "qcgd,kcd->cgqk", grouped_heads, key_rows, preferred_element_type=jnp.float32
    ) * HEAD_DIM ** (-0.5)
    allowed = (segment[:, None] == segment[None, :]) & (position[None, :] <= position[:, None])
    sink_score_logit = sinks.reshape(local_kv, head_group, 1, 1)
    masked = jnp.where(allowed[None, None], scores, -jnp.inf)
    top = jnp.maximum(jnp.max(masked, axis=-1, keepdims=True), sink_score_logit)
    expo = jnp.where(allowed[None, None], jnp.exp(scores - top), 0.0)
    denom = jnp.sum(expo, axis=-1, keepdims=True) + jnp.exp(sink_score_logit - top)
    probs = (expo / denom).astype(jnp.bfloat16)
    attended = jnp.einsum("cgqk,kcd->qcgd", probs, value_rows, preferred_element_type=jnp.float32)
    attended = attended.reshape(item_count, q_width).astype(jnp.bfloat16)
    head_term = jnp.dot(attended, w_out, preferred_element_type=jnp.float32).astype(jnp.bfloat16)
    n_y = lax.axis_size("y")
    n_c = lax.axis_size("c")
    head_term = head_term.reshape(n_y, n_c, tok_rows, model_width).transpose(1, 0, 2, 3)
    on_chip = lax.psum_scatter(head_term, "c", scatter_dimension=0, tiled=True)
    attn_sum = (
        lax.psum_scatter(
            on_chip.reshape(n_y, tok_rows, model_width), "y", scatter_dimension=0, tiled=True
        )
        .reshape(tok_rows, model_width)
        .astype(jnp.float32)
    )
    residual = (tokens.astype(jnp.float32) + attn_sum).astype(jnp.bfloat16)
    normed2 = rms_norm(residual.astype(jnp.float32), ffn_gain).astype(jnp.bfloat16)
    logits = jnp.dot(normed2, router, preferred_element_type=jnp.float32)
    picked = jnp.take_along_axis(logits, routes, axis=1)
    weights = jax.nn.softmax(picked, axis=-1)
    flat_routes = routes.reshape(-1)
    expert_ids = jnp.arange(EXPERTS, dtype=jnp.int32)
    onehot_route = (flat_routes[:, None] == expert_ids[None, :]).astype(jnp.int32)
    rank = jnp.cumsum(onehot_route, axis=0) - 1
    slot_rank = jnp.sum(onehot_route * rank, axis=1)
    flat_slot = flat_routes * CAP + slot_rank
    slot_ids = jnp.arange(EXPERTS * CAP, dtype=jnp.int32)
    dispatch_table = (slot_ids[:, None] == flat_slot[None, :]).astype(jnp.bfloat16)
    repeated = jnp.repeat(normed2, TOPK, axis=0)
    packed = jnp.dot(dispatch_table, repeated, preferred_element_type=jnp.float32).astype(
        jnp.bfloat16
    )
    halves = n_y // (EXPERTS // lax.axis_size("req"))
    send_rows = jnp.broadcast_to(
        packed.reshape(EXPERTS, 1, CAP, model_width), (EXPERTS, halves, CAP, model_width)
    ).reshape(EXPERTS * halves, CAP, model_width)
    received = lax.all_to_all(send_rows, ("req", "y"), split_axis=0, concat_axis=0, tiled=True)
    both = lax.all_gather(received, "c", axis=0, tiled=False)
    flat_rows = both.reshape(-1, model_width)
    gate = jnp.dot(flat_rows, expert_gate[0], preferred_element_type=jnp.float32)
    up_val = jnp.dot(flat_rows, expert_up[0], preferred_element_type=jnp.float32)
    hidden = ((up_val + 1.0) * gate * jax.nn.sigmoid(1.702 * gate)).astype(jnp.bfloat16)
    slice_out = jnp.dot(hidden, expert_down[0], preferred_element_type=jnp.float32).astype(
        jnp.bfloat16
    )
    swapped = lax.all_to_all(
        slice_out.reshape(both.shape), "c", split_axis=0, concat_axis=0, tiled=True
    )
    chip_sum = swapped.astype(jnp.float32).sum(axis=0).astype(jnp.bfloat16)
    returned = lax.all_to_all(chip_sum, ("req", "y"), split_axis=0, concat_axis=0, tiled=True)
    summed = returned.astype(jnp.float32).reshape(EXPERTS, halves, CAP, model_width).sum(axis=1)
    summed = summed.reshape(EXPERTS * CAP, model_width)
    picked_rows = jnp.take(summed, flat_slot, axis=0).reshape(tok_rows, TOPK, model_width)
    moe_sum = jnp.sum(weights[:, :, None] * picked_rows, axis=1)
    return (residual.astype(jnp.float32) + moe_sum).astype(jnp.bfloat16)


def solution(mesh):
    n_req, n_exp = mesh.devices.shape
    fine = jax.sharding.Mesh(mesh.devices.reshape(n_req, n_exp // 2, 2), ("req", "y", "c"))
    tok = ("req", "y", "c")
    return jax.shard_map(
        per_device,
        mesh=fine,
        in_specs=(
            P(tok, None),
            P(),
            P(None, ("y", "c")),
            P(None, ("y", "c")),
            P(None, ("y", "c")),
            P(("y", "c")),
            P(("y", "c"), None),
            P(),
            P(),
            P(tok, None),
            P("req", None),
            P(tok, None, None),
            P(tok, None, None),
            P(tok, None, None),
        ),
        out_specs=P(tok, None),
        check_vma=False,
    )
```

profile of v0, /device:TPU:10, one launch (start us, length us, event | category | flops | bytes accessed | tf_op | source)
XLA Modules:
  0.0 604.9 jit_solution(8165540641719783037)
XLA Ops:
  6.5 1.4 fusion.19
  8.0 2.1 fusion.21
  10.1 33.6 %all-gather.8.cloned.1.call-done = bf16[384,2880]{1,0:T(8,128)(2,1)} async-done(((bf16[96,2880]{1,0:T(8,128)(2,1)}), bf16[384,2880]{1,0:T(8,128)(2,1)}) %all-gather.8.cloned.1.call-update) | async-done | bytes 2211856 | tf_op jit(solution)/shard_map/all_gather | solution.py:57
  43.8 4.6 copy.109
  48.8 1.1 multiply_cosine_fusion
  50.2 13.1 %all-gather.6.cloned.1.call-done = bf16[4,192,2880]{2,1,0:T(8,128)(2,1)} async-done(((bf16[4,96,2880]{2,1,0:T(8,128)(2,1)}), bf16[4,192,2880]{2,1,0:T(8,128)(2,1)}) %all-gather.6.cloned.1.call-update) | async-done | bytes 4423696 | tf_op jit(solution)/shard_map/all_gather | solution.py:58
  63.4 3.9 convolution_bitcast_fusion
  67.8 4.5 fusion.59
  72.5 8.1 %fusion = (f32[8,768]{1,0:T(8,128)S(1)}, f32[768,768,8]{1,0,2:T(8,128)}) fusion(pred[768,768]{0,1:T(8,128)(4,1)S(1)} %fusion.13, bf16[768,8,32]{0,2,1:T(8,128)(2,1)S(1)} %get-tuple-element.10, bf16[768,8,32]{0,2,1:T(8,128)(2,1)S(1)} %get-tuple-element.9, bf16[768,32]{0,1:T(8,128)(2,1)S(1)} %get-tuple-element.12, bf16[768,32]{0,1:T(8,128)(2,1)S(1)} %get-tuple-element.11), kind=kOutput, calls=%fused_computation.4 | convolution fusion | flops 619898880 | bytes 20373504 | tf_op jit(solution)/shard_map/qcgd,kcd->cgqk/dot_general | solution.py:91
  81.3 0.7 broadcast_maximum_fusion
  82.0 10.8 %fusion.3 = f32[8,768]{1,0:T(8,128)} fusion(f32[768,768,8]{1,0,2:T(8,128)} %get-tuple-element.16, f32[8,768]{1,0:T(8,128)} %broadcast_maximum_fusion, pred[768,768]{0,1:T(8,128)(4,1)S(1)} %fusion.13), kind=kLoop, calls=%fused_computation.8 | loop fusion | flops 18868224 | bytes 19513344 | tf_op jit(solution)/shard_map/reduce_sum | solution.py:99
  92.8 1.4 exponential_add_fusion
  94.2 14.4 %fusion.16 = bf16[64,8,768]{2,0,1:T(8,128)(2,1)} fusion(f32[8,768]{1,0:T(8,128)} %exponential_add_fusion, f32[8,768]{1,0:T(8,128)} %broadcast_maximum_fusion, f32[768,768,8]{1,0,2:T(8,128)} %get-tuple-element.16, pred[768,768]{0,1:T(8,128)(4,1)S(1)} %fusion.13, bf16[768,2880]{1,0:T(8,128)(2,1)} %bitcast.132, bf16[2880,64]{0,1:T(8,128)(2,1)} %param.18), kind=kOutput, calls=%fused_computation.31 | convolution fusion | flops 911130624 | bytes 25092096 | tf_op jit(solution)/shard_map/cgqk,kcd->qcgd/dot_general | solution.py:101
  108.6 5.6 convolution_convert_fusion.1
  114.2 6.6 %copy.112 = bf16[768,2880]{1,0:T(8,128)(2,1)} copy(bf16[768,2880]{0,1:T(8,128)(2,1)} %convolution_convert_fusion.1) | data formatting | bytes 8847360 | tf_op jit(solution)/shard_map/convert_element_type | solution.py:103
  121.5 35.2 %all-reduce.3.cloned.1.call-done = bf16[2,4,96,2880]{3,2,0,1:T(8,128)(2,1)} async-done(((bf16[2,4,96,2880]{3,2,0,1:T(8,128)(2,1)}), bf16[2,4,96,2880]{3,2,0,1:T(8,128)(2,1)}) %all-reduce.3.cloned.1.call-update) | async-done | bytes 4423696
  156.7 3.9 dynamic-slice_bitcast_fusion
  161.0 0.9 reduce-window.11
  162.3 29.5 %reduce-scatter.3.cloned.1.call-done = bf16[1,96,2880]{2,1,0:T(8,128)(2,1)} async-done(((bf16[4,96,2880]{2,1,0:T(8,128)(2,1)}), bf16[1,96,2880]{2,1,0:T(8,128)(2,1)}) %reduce-scatter.3.cloned.1.call-update) | async-done | bytes 552976 | tf_op jit(solution)/shard_map/reduce_scatter | solution.py:109
  191.8 1.3 fusion.23
  193.2 1.3 fusion.25
  195.0 2.4 reshape.430
  197.5 4.7 convolution_convert_fusion.2
  202.2 4.4 broadcast_in_dim.41
  206.6 2.3 broadcast_in_dim.42
  208.8 92.3 %all_to_all.15 = bf16[64,14,2880]{2,1,0:T(8,128)(2,1)S(1)} all-to-all(bf16[64,14,2880]{2,1,0:T(8,128)(2,1)S(1)} %bitcast.129), channel_id=1, replica_groups=mesh['req'=16,'y'=4,'c'=2] {'req','y'}, dimensions={0} | all-to-all | bytes 10321920 | tf_op jit(solution)/shard_map/all_to_all | solution.py:136
  301.2 3.4 copy.121
  304.7 23.4 %all-gather.10.cloned.1.call-done = bf16[128,14,2880]{2,0,1:T(8,128)(2,1)} async-done(((bf16[64,14,2880]{2,0,1:T(8,128)(2,1)}), bf16[128,14,2880]{2,0,1:T(8,128)(2,1)}) %all-gather.10.cloned.1.call-update) | async-done | bytes 10321936 | tf_op jit(solution)/shard_map/all_gather | solution.py:137
  328.1 13.6 %copy.122 = bf16[128,14,2880]{2,1,0:T(8,128)(2,1)} copy(bf16[128,14,2880]{2,0,1:T(8,128)(2,1)} %all-gather.10.cloned.1.call-done) | data formatting | bytes 20643840 | tf_op jit(solution)/shard_map/all_gather | solution.py:137
  341.7 15.4 %reshape.432 = bf16[1792,2880]{1,0:T(8,128)(2,1)} reshape(bf16[128,14,2880]{2,1,0:T(8,128)(2,1)} %copy.122) | data formatting | bytes 20643840 | tf_op jit(solution)/shard_map/reshape | solution.py:138
  357.1 14.6 %fusion.7 = f32[1792,720]{0,1:T(8,128)} fusion(bf16[1792,2880]{1,0:T(8,128)(2,1)} %reshape.432, bf16[1,2880,720]{1,2,0:T(8,128)(2,1)} %param.25), kind=kOutput, calls=%fused_computation.18 | convolution fusion | flops 7431782400 | bytes 19630080 | tf_op jit(solution)/shard_map/dot_general | solution.py:139
  371.7 27.3 %convolution_convert_fusion = bf16[1792,2880]{0,1:T(8,128)(2,1)} fusion(bf16[1,720,2880]{2,1,0:T(8,128)(2,1)} %param.27, f32[1792,720]{0,1:T(8,128)} %fusion.7, bf16[1792,2880]{1,0:T(8,128)(2,1)} %reshape.432, bf16[1,2880,720]{1,2,0:T(8,128)(2,1)} %param.26), kind=kOutput, calls=%fused_computation.10 | convolution fusion | flops 14879047680 | bytes 34099200 | tf_op jit(solution)/shard_map/dot_general | solution.py:142
  399.0 14.5 %copy.123 = bf16[1792,2880]{1,0:T(8,128)(2,1)} copy(bf16[1792,2880]{0,1:T(8,128)(2,1)} %convolution_convert_fusion) | data formatting | bytes 20643840 | tf_op jit(solution)/shard_map/convert_element_type | solution.py:142
  413.4 14.4 %reshape.433 = bf16[2,64,14,2880]{3,2,1,0:T(8,128)(2,1)} reshape(bf16[1792,2880]{1,0:T(8,128)(2,1)} %copy.123) | data formatting | bytes 20643840 | tf_op jit(solution)/shard_map/reshape | solution.py:146
  427.8 10.7 %copy.124 = bf16[2,64,14,2880]{3,1,2,0:T(8,128)(2,1)S(1)} copy(bf16[2,64,14,2880]{3,2,1,0:T(8,128)(2,1)} %reshape.433) | data formatting | bytes 20643840 | tf_op jit(solution)/shard_map/reshape | solution.py:146
  438.5 14.0 %all_to_all.16 = bf16[2,64,14,2880]{3,1,2,0:T(8,128)(2,1)} all-to-all(bf16[2,64,14,2880]{3,1,2,0:T(8,128)(2,1)S(1)} %copy.124), channel_id=1, replica_groups=mesh['req'=16,'y'=4,'c'=2] {'c'}, dimensions={0} | all-to-all | bytes 20643840 | tf_op jit(solution)/shard_map/all_to_all | solution.py:145
  452.5 9.7 %reduce_sum.105 = bf16[64,14,2880]{2,0,1:T(8,128)(2,1)} reduce(bf16[2,64,14,2880]{3,1,2,0:T(8,128)(2,1)} %all_to_all.16, bf16[]{:T(256)} %constant.70.clone.1), dimensions={0}, to_apply=%region_14.15 | reduce | flops 2580480 | bytes 15482882 | tf_op jit(solution)/shard_map/reduce_sum | solution.py:148
  462.1 8.0 %copy.125 = bf16[64,14,2880]{2,1,0:T(8,128)(2,1)} copy(bf16[64,14,2880]{2,0,1:T(8,128)(2,1)} %reduce_sum.105) | data formatting | bytes 10321920 | tf_op jit(solution)/shard_map/reduce_sum | solution.py:148
  470.1 11.1 %all-to-all-start.2 = ((bf16[64,14,2880]{2,1,0:T(8,128)(2,1)}), bf16[64,14,2880]{2,1,0:T(8,128)(2,1)}, u32[]{:S(2)}, u32[]{:S(2)}) async-start(bf16[64,14,2880]{2,1,0:T(8,128)(2,1)} %copy.125), calls=%async_computation.3 | async-start | bytes 12058624 | tf_op jit(solution)/shard_map/all_to_all | solution.py:149
  482.4 2.9 gather_fusion.1
  485.5 0.7 copy.115
  486.2 76.9 %all-to-all-done.2 = bf16[64,14,2880]{2,1,0:T(8,128)(2,1)} async-done(((bf16[64,14,2880]{2,1,0:T(8,128)(2,1)}), bf16[64,14,2880]{2,1,0:T(8,128)(2,1)}, u32[]{:S(2)}, u32[]{:S(2)}) %all-to-all-start.2) | async-done | bytes 5160992 | tf_op jit(solution)/shard_map/all_to_all | solution.py:149
  563.1 7.0 %convert_reduce_fusion = f32[32,14,2880]{2,1,0:T(8,128)} fusion(bf16[64,14,2880]{2,1,0:T(8,128)(2,1)} %all-to-all-done.2), kind=kLoop, calls=%fused_computation.9 | loop fusion | flops 3870720 | bytes 10321920 | tf_op jit(solution)/shard_map/reduce_sum | solution.py:150
  570.1 5.7 reshape.436
  575.8 9.0 %gather_fusion = f32[384,2880]{1,0:T(8,128)} fusion(f32[448,2880]{1,0:T(8,128)} %reshape.436, s32[1024]{0:T(1024)S(1)} %pad_clamp_fusion), kind=kCustom, calls=%fused_computation | custom fusion | bytes 8848896 | tf_op jit(solution)/shard_map/jit(_take)/gather | solution.py:152
  584.8 5.5 gather.12
  590.4 6.5 %multiply_reduce_fusion = f32[96,2880]{1,0:T(8,128)S(1)} fusion(f32[96,4,2880]{2,1,0:T(4,128)} %gather.12, f32[96,4]{1,0:T(8,128)} %copy.115, pred[96,4]{1,0:T(8,128)(4,1)S(1)} %copy.120), kind=kLoop, calls=%fused_computation.15 | loop fusion | flops 3041280 | bytes 5531520 | tf_op jit(solution)/shard_map/reduce_sum | solution.py:153
  596.9 1.0 fusion.26
  (76 shorter events, 5.4 us)
Async XLA Ops:
  6.5 102.1 %copy-start = (bf16[512,2880]{0,1:T(8,128)(2,1)S(1)}, bf16[512,2880]{0,1:T(8,128)(2,1)}, u32[]{:S(2)}) copy-start(bf16[512,2880]{0,1:T(8,128)(2,1)} %param.20) | copy-start | bytes 8847364
  6.5 37.2 %all-gather.8.cloned.1.call-start = ((), (), s32[]{:S(2)}) async-start(), calls=%async_computation.6 | async-start | bytes 2826240 | tf_op jit(solution)/shard_map/all_gather | solution.py:57
  10.0 38.4 %copy-start.12 = (s32[1,6]{1,0:T(1,128)S(1)}, s32[1,6]{1,0:T(1,128)}, u32[]{:S(2)}) copy-start(s32[1,6]{1,0:T(1,128)} %param.24) | copy-start | bytes 76
  10.1 53.3 %all-gather.6.cloned.1.call-start = ((), (), s32[]{:S(2)}) async-start(), calls=%async_computation.4 | async-start | bytes 6782976 | tf_op jit(solution)/shard_map/all_gather | solution.py:58
  43.8 112.9 %all-reduce.3.cloned.1.call-start = ((), (), s32[]{:S(2)}) async-start(), calls=%async_computation.8 | async-start | bytes 9043968
  63.4 4.4 copy-start.4
  67.7 4.6 copy-start.5
  67.7 4.6 copy-start.6
  72.5 8.8 %copy-start.11 = (f32[8]{0:T(128)S(1)}, f32[8]{0:T(128)}, u32[]{:S(2)}) copy-start(f32[8]{0:T(128)} %param.19) | copy-start | bytes 100
  80.7 0.6 copy-start.7
  114.2 6.7 %copy-start.13 = (u32[128]{0:T(128)S(1)}, u32[128]{0:T(128)}, u32[]{:S(2)}) copy-start(u32[128]{0:T(128)} %constant.92) | copy-start | bytes 1540
  120.8 39.8 %copy-start.9 = (s32[96,4]{0,1:T(4,128)S(1)}, s32[96,4]{0,1:T(4,128)}, u32[]{:S(2)}) copy-start(s32[96,4]{0,1:T(4,128)} %param.23) | copy-start | bytes 4612
  120.8 71.0 %copy-start.2 = (bf16[96,2880]{1,0:T(8,128)(2,1)S(1)}, bf16[96,2880]{1,0:T(8,128)(2,1)}, u32[]{:S(2)}) copy-start(bf16[96,2880]{1,0:T(8,128)(2,1)} %param.14) | copy-start | bytes 1658884
  120.8 72.3 %copy-start.10 = (f32[2880]{0:T(1024)S(1)}, f32[2880]{0:T(1024)}, u32[]{:S(2)}) copy-start(f32[2880]{0:T(1024)} %param.21) | copy-start | bytes 34564
  120.9 70.9 %reduce-scatter.3.cloned.1.call-start = ((), (), s32[]{:S(2)}) async-start(), calls=%async_computation.5 | async-start | bytes 2826240 | tf_op jit(solution)/shard_map/reduce_scatter | solution.py:109
  160.6 167.5 %all-gather.10.cloned.1.call-start = ((), (), s32[]{:S(2)}) async-start(), calls=%async_computation.7 | async-start | bytes 15826944 | tf_op jit(solution)/shard_map/all_gather | solution.py:137
  470.1 11.9 %copy-start.8 = (bf16[2880,32]{0,1:T(8,128)(2,1)S(1)}, bf16[2880,32]{0,1:T(8,128)(2,1)}, u32[]{:S(2)}) copy-start(bf16[2880,32]{0,1:T(8,128)(2,1)} %param.22) | copy-start | bytes 552964
  470.1 93.0 %all-to-all-start.2 = ((bf16[64,14,2880]{2,1,0:T(8,128)(2,1)}), bf16[64,14,2880]{2,1,0:T(8,128)(2,1)}, u32[]{:S(2)}, u32[]{:S(2)}) async-start(bf16[64,14,2880]{2,1,0:T(8,128)(2,1)} %copy.125), calls=%async_computation.3 | async-start | bytes 12058624 | tf_op jit(solution)/shard_map/all_to_all | solution.py:149
  584.8 13.1 %copy-start.1 = (bf16[512,2880]{0,1:T(8,128)(2,1)S(1)}, bf16[512,2880]{0,1:T(8,128)(2,1)}, u32[]{:S(2)}) copy-start(bf16[512,2880]{0,1:T(8,128)(2,1)} %param.20) | copy-start | bytes 8847364
  590.4 6.5 %copy-start.3 = (bf16[1,96,2880]{2,1,0:T(8,128)(2,1)S(1)}, bf16[1,96,2880]{2,1,0:T(8,128)(2,1)}, u32[]{:S(2)}) copy-start(bf16[1,96,2880]{2,1,0:T(8,128)(2,1)} %reduce-scatter.3.cloned.1.call-done) | copy-start | bytes 1658884
Sparse Core Ops, SparseCore 0:
  10.2 33.5 all-gather.7
  45.4 17.8 all-gather.5
  120.9 35.7 all-reduce.2
  160.7 31.0 reduce-scatter.2
  304.8 23.2 all-gather.9
where the time goes:
time: 614 us; the launch traced here: 605 us
  waiting for transfers between devices  212 us (35%)
  local copies, waits for them, and re-layouts  131 us (21%)
  blocking collectives  106 us (17%)
  matrix products  83.4 us (14%)
  other arithmetic  46.8 us (8%)
  between operations  13.9 us (2%)
  starting transfers between devices  11.3 us (2%)
    all_to_all x1, blocking collectives, per_device(): lax.all_to_all(send_rows, ('req', 'y'), split_axis=0, concat_axis=0, tile...  92.3 us
    all_to_all x1, waiting for transfers between devices, per_device(): lax.all_to_all(chip_sum, ('req', 'y'), split_axis=0, concat_axis=0, tiled...  76.9 us
    unnamed x6, waiting for transfers between devices  35.3 us
    all_gather x1, waiting for transfers between devices, per_device(): by_chip = lax.all_gather(normed_input, 'y', axis=0, tiled=False)  33.6 us
    reduce_scatter x1, waiting for transfers between devices, per_device(): lax.psum_scatter(on_chip.reshape(n_y, tok_rows, model_width), 'y', scatte...  29.5 us
    dot_general x1, matrix products, per_device(): jnp.dot(hidden, expert_down[0], preferred_element_type=jnp.float32)  27.3 us
    reshape x2, local copies, waits for them, and re-layouts, per_device(): slice_out.reshape(both.shape)  25.1 us
    all_gather x1, waiting for transfers between devices, per_device(): both = lax.all_gather(received, 'c', axis=0, tiled=False)  23.4 us
  transfers between devices with their start and end apart: 6, of which 6 were waited for; matrix products, arithmetic and copies ran while one was open for 2% of the time, Pallas kernels for 0%

commit v1 on v0

--- a/solution.py
+++ b/solution.py
@@ -55,7 +55,9 @@
     head_group = QUERY_HEADS // KEY_VALUE_HEADS
     normed_input = rms_norm(tokens.astype(jnp.float32), attn_gain).astype(jnp.bfloat16)
     by_chip = lax.all_gather(normed_input, "y", axis=0, tiled=False)
-    piece = lax.all_gather(by_chip, "c", axis=1, tiled=True).reshape(-1, model_width)
+    piece = jnp.concatenate(
+        lax.all_to_all(jnp.stack([by_chip] * lax.axis_size("c")), "c", 0, 0), axis=1
+    ).reshape(-1, model_width)
     projected = jnp.concatenate(
         [
             jnp.dot(piece, w_query, preferred_element_type=jnp.float32),

time: 614 us -> 586 us (0.954)
  waiting for transfers between devices: 212 us -> 193 us
    all_gather x1 -> x0, waiting for transfers between devices: 13.1 us -> none  [per_device(): lax.all_gather(by_chip, 'c', axis=1, tiled=True).reshape(-1, model_width)]
    all_to_all x1, blocking collectives: 92.3 us -> 80.2 us  [per_device(): lax.all_to_all(send_rows, ('req', 'y'), split_axis=0, concat_axis=0, tile...]
    all_to_all x0 -> x1, blocking collectives: none -> 7.52 us  [per_device(): lax.all_to_all(jnp.stack([by_chip] * lax.axis_size('c')), 'c', 0, 0)]
    all_gather x1, waiting for transfers between devices: 33.6 us -> 27.3 us  [per_device(): by_chip = lax.all_gather(normed_input, 'y', axis=0, tiled=False)]
    unnamed x6 -> x5, waiting for transfers between devices: 35.3 us -> 35 us
  transfers between devices with their start and end apart: 6 -> 5, of which waited for: 6 -> 5; matrix products, arithmetic and copies ran while one was open for 2% -> 2% of each run, Pallas kernels for 0% -> 0%
where the time goes in v1:
time: 586 us; the launch traced here: 582 us
  waiting for transfers between devices  193 us (33%)
  local copies, waits for them, and re-layouts  133 us (23%)
  blocking collectives  102 us (17%)
  matrix products  79.3 us (14%)
  other arithmetic  49.6 us (8%)
  between operations  13.7 us (2%)
  starting transfers between devices  11.2 us (2%)
    all_to_all x1, blocking collectives, per_device(): lax.all_to_all(send_rows, ('req', 'y'), split_axis=0, concat_axis=0, tile...  80.2 us
    all_to_all x1, waiting for transfers between devices, per_device(): lax.all_to_all(chip_sum, ('req', 'y'), split_axis=0, concat_axis=0, tiled...  76.9 us
    unnamed x5, waiting for transfers between devices  35 us
    reduce_scatter x1, waiting for transfers between devices, per_device(): lax.psum_scatter(on_chip.reshape(n_y, tok_rows, model_width), 'y', scatte...  29.5 us
    dot_general x1, matrix products, per_device(): jnp.dot(hidden, expert_down[0], preferred_element_type=jnp.float32)  27.7 us
    all_gather x1, waiting for transfers between devices, per_device(): by_chip = lax.all_gather(normed_input, 'y', axis=0, tiled=False)  27.3 us
    reshape x2, local copies, waits for them, and re-layouts, per_device(): slice_out.reshape(both.shape)  25.1 us
    all_gather x1, waiting for transfers between devices, per_device(): both = lax.all_gather(received, 'c', axis=0, tiled=False)  24.2 us
  transfers between devices with their start and end apart: 5, of which 5 were waited for; matrix products, arithmetic and copies ran while one was open for 2% of the time, Pallas kernels for 0%

profile of v1, /device:TPU:10, one launch (start us, length us, event | category | flops | bytes accessed | tf_op | source)
XLA Modules:
  0.0 581.6 jit_solution(6751072774722703746)
XLA Ops:
  6.5 1.4 fusion.19
  8.0 2.1 fusion.21
  10.1 4.6 copy.117
  15.0 1.1 multiply_cosine_fusion
  16.5 27.3 %all-gather.5.cloned.1.call-done = bf16[384,2880]{1,0:T(8,128)(2,1)} async-done(((bf16[96,2880]{1,0:T(8,128)(2,1)}), bf16[384,2880]{1,0:T(8,128)(2,1)}) %all-gather.5.cloned.1.call-update) | async-done | bytes 2211856 | tf_op jit(solution)/shard_map/all_gather | solution.py:57
  43.8 2.8 pad_maximum_fusion
  46.6 7.5 %all_to_all.20 = bf16[2,4,96,2880]{3,2,1,0:T(8,128)(2,1)S(1)} all-to-all(bf16[2,4,96,2880]{3,2,1,0:T(8,128)(2,1)S(1)} %pad_maximum_fusion), channel_id=1, replica_groups=mesh['req'=16,'y'=4,'c'=2] {'c'}, dimensions={0} | all-to-all | bytes 8847360 | tf_op jit(solution)/shard_map/all_to_all | solution.py:59
  55.1 1.4 convolution_bitcast_fusion
  56.9 1.0 copy-done.5
  58.0 2.7 fusion.59
  60.9 8.1 %fusion = (f32[8,768]{1,0:T(8,128)S(1)}, f32[768,768,8]{1,0,2:T(8,128)}) fusion(pred[768,768]{0,1:T(8,128)(4,1)S(1)} %fusion.13, bf16[768,8,32]{0,2,1:T(8,128)(2,1)S(1)} %get-tuple-element.10, bf16[768,8,32]{0,2,1:T(8,128)(2,1)S(1)} %get-tuple-element.9, bf16[768,32]{0,1:T(8,128)(2,1)S(1)} %get-tuple-element.12, bf16[768,32]{0,1:T(8,128)(2,1)S(1)} %get-tuple-element.11), kind=kOutput, calls=%fused_computation.4 | convolution fusion | flops 619898880 | bytes 20373504 | tf_op jit(solution)/shard_map/qcgd,kcd->cgqk/dot_general | solution.py:93
  70.3 10.8 %fusion.3 = f32[8,768]{1,0:T(8,128)} fusion(f32[768,768,8]{1,0,2:T(8,128)} %get-tuple-element.16, f32[8,768]{1,0:T(8,128)} %broadcast_maximum_fusion, pred[768,768]{0,1:T(8,128)(4,1)S(1)} %fusion.13), kind=kLoop, calls=%fused_computation.8 | loop fusion | flops 18868224 | bytes 19513344 | tf_op jit(solution)/shard_map/reduce_sum | solution.py:101
  81.1 1.4 exponential_add_fusion
  82.5 14.3 %fusion.16 = bf16[64,8,768]{2,0,1:T(8,128)(2,1)} fusion(f32[8,768]{1,0:T(8,128)} %exponential_add_fusion, f32[8,768]{1,0:T(8,128)} %broadcast_maximum_fusion, f32[768,768,8]{1,0,2:T(8,128)} %get-tuple-element.16, pred[768,768]{0,1:T(8,128)(4,1)S(1)} %fusion.13, bf16[768,2880]{1,0:T(8,128)(2,1)} %bitcast.133, bf16[2880,64]{0,1:T(8,128)(2,1)} %param.18), kind=kOutput, calls=%fused_computation.32 | convolution fusion | flops 911130624 | bytes 25092096 | tf_op jit(solution)/shard_map/cgqk,kcd->qcgd/dot_general | solution.py:103
  96.9 5.6 convolution_convert_fusion.1
  102.5 6.6 %copy.120 = bf16[768,2880]{1,0:T(8,128)(2,1)} copy(bf16[768,2880]{0,1:T(8,128)(2,1)} %convolution_convert_fusion.1) | data formatting | bytes 8847360 | tf_op jit(solution)/shard_map/convert_element_type | solution.py:105
  109.8 34.9 %all-reduce.3.cloned.1.call-done = bf16[2,4,96,2880]{3,2,0,1:T(8,128)(2,1)} async-done(((bf16[2,4,96,2880]{3,2,0,1:T(8,128)(2,1)}), bf16[2,4,96,2880]{3,2,0,1:T(8,128)(2,1)}) %all-reduce.3.cloned.1.call-update) | async-done | bytes 4423696
  144.7 3.9 dynamic-slice_bitcast_fusion
  149.0 0.9 reduce-window.11
  150.3 29.5 %reduce-scatter.3.cloned.1.call-done = bf16[1,96,2880]{2,1,0:T(8,128)(2,1)} async-done(((bf16[4,96,2880]{2,1,0:T(8,128)(2,1)}), bf16[1,96,2880]{2,1,0:T(8,128)(2,1)}) %reduce-scatter.3.cloned.1.call-update) | async-done | bytes 552976 | tf_op jit(solution)/shard_map/reduce_scatter | solution.py:111
  179.8 1.3 fusion.23
  181.2 1.3 fusion.25
  183.0 2.4 reshape.430
  185.5 4.7 convolution_convert_fusion.2
  190.2 4.4 broadcast_in_dim.41
  194.6 2.3 broadcast_in_dim.42
  196.9 80.2 %all_to_all.21 = bf16[64,14,2880]{2,1,0:T(8,128)(2,1)S(1)} all-to-all(bf16[64,14,2880]{2,1,0:T(8,128)(2,1)S(1)} %bitcast.130), channel_id=1, replica_groups=mesh['req'=16,'y'=4,'c'=2] {'req','y'}, dimensions={0} | all-to-all | bytes 10321920 | tf_op jit(solution)/shard_map/all_to_all | solution.py:138
  277.1 3.4 copy.129
  280.5 24.2 %all-gather.7.cloned.1.call-done = bf16[128,14,2880]{2,0,1:T(8,128)(2,1)} async-done(((bf16[64,14,2880]{2,0,1:T(8,128)(2,1)}), bf16[128,14,2880]{2,0,1:T(8,128)(2,1)}) %all-gather.7.cloned.1.call-update) | async-done | bytes 10321936 | tf_op jit(solution)/shard_map/all_gather | solution.py:139
  304.7 13.6 %copy.130 = bf16[128,14,2880]{2,1,0:T(8,128)(2,1)} copy(bf16[128,14,2880]{2,0,1:T(8,128)(2,1)} %all-gather.7.cloned.1.call-done) | data formatting | bytes 20643840 | tf_op jit(solution)/shard_map/all_gather | solution.py:139
  318.3 15.4 %reshape.432 = bf16[1792,2880]{1,0:T(8,128)(2,1)} reshape(bf16[128,14,2880]{2,1,0:T(8,128)(2,1)} %copy.130) | data formatting | bytes 20643840 | tf_op jit(solution)/shard_map/reshape | solution.py:140
  333.7 14.6 %fusion.7 = f32[1792,720]{0,1:T(8,128)} fusion(bf16[1792,2880]{1,0:T(8,128)(2,1)} %reshape.432, bf16[1,2880,720]{1,2,0:T(8,128)(2,1)} %param.25), kind=kOutput, calls=%fused_computation.19 | convolution fusion | flops 7431782400 | bytes 19630080 | tf_op jit(solution)/shard_map/dot_general | solution.py:141
  348.3 27.7 %convolution_convert_fusion = bf16[1792,2880]{0,1:T(8,128)(2,1)} fusion(bf16[1,720,2880]{2,1,0:T(8,128)(2,1)} %param.27, f32[1792,720]{0,1:T(8,128)} %fusion.7, bf16[1792,2880]{1,0:T(8,128)(2,1)} %reshape.432, bf16[1,2880,720]{1,2,0:T(8,128)(2,1)} %param.26), kind=kOutput, calls=%fused_computation.10 | convolution fusion | flops 14879047680 | bytes 34099200 | tf_op jit(solution)/shard_map/dot_general | solution.py:144
  376.0 14.5 %copy.131 = bf16[1792,2880]{1,0:T(8,128)(2,1)} copy(bf16[1792,2880]{0,1:T(8,128)(2,1)} %convolution_convert_fusion) | data formatting | bytes 20643840 | tf_op jit(solution)/shard_map/convert_element_type | solution.py:144
  390.5 14.4 %reshape.433 = bf16[2,64,14,2880]{3,2,1,0:T(8,128)(2,1)} reshape(bf16[1792,2880]{1,0:T(8,128)(2,1)} %copy.131) | data formatting | bytes 20643840 | tf_op jit(solution)/shard_map/reshape | solution.py:148
  404.9 10.7 %copy.132 = bf16[2,64,14,2880]{3,1,2,0:T(8,128)(2,1)S(1)} copy(bf16[2,64,14,2880]{3,2,1,0:T(8,128)(2,1)} %reshape.433) | data formatting | bytes 20643840 | tf_op jit(solution)/shard_map/reshape | solution.py:148
  415.5 13.9 %all_to_all.22 = bf16[2,64,14,2880]{3,1,2,0:T(8,128)(2,1)} all-to-all(bf16[2,64,14,2880]{3,1,2,0:T(8,128)(2,1)S(1)} %copy.132), channel_id=1, replica_groups=mesh['req'=16,'y'=4,'c'=2] {'c'}, dimensions={0} | all-to-all | bytes 20643840 | tf_op jit(solution)/shard_map/all_to_all | solution.py:147
  429.5 9.7 %reduce_sum.105 = bf16[64,14,2880]{2,0,1:T(8,128)(2,1)} reduce(bf16[2,64,14,2880]{3,1,2,0:T(8,128)(2,1)} %all_to_all.22, bf16[]{:T(256)} %constant.70.clone.1), dimensions={0}, to_apply=%region_14.15 | reduce | flops 2580480 | bytes 15482882 | tf_op jit(solution)/shard_map/reduce_sum | solution.py:150
  439.1 8.0 %copy.133 = bf16[64,14,2880]{2,1,0:T(8,128)(2,1)} copy(bf16[64,14,2880]{2,0,1:T(8,128)(2,1)} %reduce_sum.105) | data formatting | bytes 10321920 | tf_op jit(solution)/shard_map/reduce_sum | solution.py:150
  447.1 11.1 %all-to-all-start.3 = ((bf16[64,14,2880]{2,1,0:T(8,128)(2,1)}), bf16[64,14,2880]{2,1,0:T(8,128)(2,1)}, u32[]{:S(2)}, u32[]{:S(2)}) async-start(bf16[64,14,2880]{2,1,0:T(8,128)(2,1)} %copy.133), calls=%async_computation.4 | async-start | bytes 12058624 | tf_op jit(solution)/shard_map/all_to_all | solution.py:151
  459.3 2.9 gather_fusion.1
  463.2 76.9 %all-to-all-done.3 = bf16[64,14,2880]{2,1,0:T(8,128)(2,1)} async-done(((bf16[64,14,2880]{2,1,0:T(8,128)(2,1)}), bf16[64,14,2880]{2,1,0:T(8,128)(2,1)}, u32[]{:S(2)}, u32[]{:S(2)}) %all-to-all-start.3) | async-done | bytes 5160992 | tf_op jit(solution)/shard_map/all_to_all | solution.py:151
  540.1 7.0 %convert_reduce_fusion = f32[32,14,2880]{2,1,0:T(8,128)} fusion(bf16[64,14,2880]{2,1,0:T(8,128)(2,1)} %all-to-all-done.3), kind=kLoop, calls=%fused_computation.9 | loop fusion | flops 3870720 | bytes 10321920 | tf_op jit(solution)/shard_map/reduce_sum | solution.py:152
  547.1 5.7 reshape.436
  552.8 9.0 %gather_fusion = f32[384,2880]{1,0:T(8,128)} fusion(f32[448,2880]{1,0:T(8,128)} %reshape.436, s32[1024]{0:T(1024)S(1)} %pad_clamp_fusion), kind=kCustom, calls=%fused_computation | custom fusion | bytes 8848896 | tf_op jit(solution)/shard_map/jit(_take)/gather | solution.py:154
  561.8 5.5 gather.12
  567.3 6.5 %multiply_reduce_fusion = f32[96,2880]{1,0:T(8,128)S(1)} fusion(f32[96,4,2880]{2,1,0:T(4,128)} %gather.12, f32[96,4]{1,0:T(8,128)} %copy.123, pred[96,4]{1,0:T(8,128)(4,1)S(1)} %copy.128), kind=kLoop, calls=%fused_computation.16 | loop fusion | flops 3041280 | bytes 5531520 | tf_op jit(solution)/shard_map/reduce_sum | solution.py:155
  573.8 1.0 fusion.26
  (80 shorter events, 7.7 us)
Async XLA Ops:
  6.5 90.3 %copy-start = (bf16[512,2880]{0,1:T(8,128)(2,1)S(1)}, bf16[512,2880]{0,1:T(8,128)(2,1)}, u32[]{:S(2)}) copy-start(bf16[512,2880]{0,1:T(8,128)(2,1)} %param.20) | copy-start | bytes 8847364
  6.5 8.2 %copy-start.14 = (s32[1,6]{1,0:T(1,128)S(1)}, s32[1,6]{1,0:T(1,128)}, u32[]{:S(2)}) copy-start(s32[1,6]{1,0:T(1,128)} %param.24) | copy-start | bytes 76
  6.5 37.2 %all-gather.5.cloned.1.call-start = ((), (), s32[]{:S(2)}) async-start(), calls=%async_computation.6 | async-start | bytes 2826240 | tf_op jit(solution)/shard_map/all_gather | solution.py:57
  10.1 134.6 %all-reduce.3.cloned.1.call-start = ((), (), s32[]{:S(2)}) async-start(), calls=%async_computation.8 | async-start | bytes 9043968
  54.1 1.0 copy-start.8
  54.4 6.2 %copy-start.2 = (bf16[4,2,96,2880]{3,2,1,0:T(8,128)(2,1)}, bf16[4,2,96,2880]{3,2,1,0:T(8,128)(2,1)S(1)}, u32[]{:S(2)}) copy-start(bf16[4,2,96,2880]{3,2,1,0:T(8,128)(2,1)S(1)} %copy.116) | copy-start | bytes 13271044
  54.4 3.5 copy-start.5
  58.0 2.7 copy-start.6
  58.0 2.7 copy-start.7
  60.9 8.8 %copy-start.13 = (f32[8]{0:T(128)S(1)}, f32[8]{0:T(128)}, u32[]{:S(2)}) copy-start(f32[8]{0:T(128)} %param.19) | copy-start | bytes 100
  69.0 0.6 copy-start.9
  102.5 6.7 %copy-start.15 = (u32[128]{0:T(128)S(1)}, u32[128]{0:T(128)}, u32[]{:S(2)}) copy-start(u32[128]{0:T(128)} %constant.92) | copy-start | bytes 1540
  109.1 39.5 %copy-start.11 = (s32[96,4]{0,1:T(4,128)S(1)}, s32[96,4]{0,1:T(4,128)}, u32[]{:S(2)}) copy-start(s32[96,4]{0,1:T(4,128)} %param.23) | copy-start | bytes 4612
  109.1 70.7 %copy-start.3 = (bf16[96,2880]{1,0:T(8,128)(2,1)S(1)}, bf16[96,2880]{1,0:T(8,128)(2,1)}, u32[]{:S(2)}) copy-start(bf16[96,2880]{1,0:T(8,128)(2,1)} %param.14) | copy-start | bytes 1658884
  109.1 72.0 %copy-start.12 = (f32[2880]{0:T(1024)S(1)}, f32[2880]{0:T(1024)}, u32[]{:S(2)}) copy-start(f32[2880]{0:T(1024)} %param.21) | copy-start | bytes 34564
  109.2 70.7 %reduce-scatter.3.cloned.1.call-start = ((), (), s32[]{:S(2)}) async-start(), calls=%async_computation.5 | async-start | bytes 2826240 | tf_op jit(solution)/shard_map/reduce_scatter | solution.py:111
  148.6 156.1 %all-gather.7.cloned.1.call-start = ((), (), s32[]{:S(2)}) async-start(), calls=%async_computation.7 | async-start | bytes 15826944 | tf_op jit(solution)/shard_map/all_gather | solution.py:139
  447.1 11.9 %copy-start.10 = (bf16[2880,32]{0,1:T(8,128)(2,1)S(1)}, bf16[2880,32]{0,1:T(8,128)(2,1)}, u32[]{:S(2)}) copy-start(bf16[2880,32]{0,1:T(8,128)(2,1)} %param.22) | copy-start | bytes 552964
  447.1 92.9 %all-to-all-start.3 = ((bf16[64,14,2880]{2,1,0:T(8,128)(2,1)}), bf16[64,14,2880]{2,1,0:T(8,128)(2,1)}, u32[]{:S(2)}, u32[]{:S(2)}) async-start(bf16[64,14,2880]{2,1,0:T(8,128)(2,1)} %copy.133), calls=%async_computation.4 | async-start | bytes 12058624 | tf_op jit(solution)/shard_map/all_to_all | solution.py:151
  561.8 13.1 %copy-start.1 = (bf16[512,2880]{0,1:T(8,128)(2,1)S(1)}, bf16[512,2880]{0,1:T(8,128)(2,1)}, u32[]{:S(2)}) copy-start(bf16[512,2880]{0,1:T(8,128)(2,1)} %param.20) | copy-start | bytes 8847364
  567.3 6.5 %copy-start.4 = (bf16[1,96,2880]{2,1,0:T(8,128)(2,1)S(1)}, bf16[1,96,2880]{2,1,0:T(8,128)(2,1)}, u32[]{:S(2)}) copy-start(bf16[1,96,2880]{2,1,0:T(8,128)(2,1)} %reduce-scatter.3.cloned.1.call-done) | copy-start | bytes 1658884
Sparse Core Ops, SparseCore 0:
  10.2 33.5 all-gather.4
  109.2 35.4 all-reduce.2
  148.7 31.0 reduce-scatter.2
  280.7 23.9 all-gather.6
